TPU v7x, 512 devices: a whole 4x4x16 slice. The times are simulated.
512 devices in a mesh: dom: 16 (over x_hi, y, core), band: 32 (over z, x_lo).
Axes of the slice: x: 4 (x_hi: 2, x_lo: 2; x = x_hi * 2 + x_lo), y: 4, z: 16, core: 2. Of those that a mesh axis runs over, the one named last changes fastest.
Arguments:
- psi: float32 [1024, 192, 2, 384], P('band', 'dom'), may hold values from -6 to 6
- potential: float32 [192, 2, 384], P('dom'), may hold values from -3 to 3
- rotation: bfloat16 [1024, 1024], replicated, may hold values from -0.1875 to 0.1875
Outputs:
- rotated: bfloat16 [1024, 192, 2, 384], P('band', 'dom')
All inputs are finite; a program needn't handle non-finite values.
Results may differ from a plain program's by a relative error of at most 0.005.
Values may be sent and summed in bfloat16 or wider, within the bound.
No kernel may reach another device: no remote copies, remote signals or barrier semaphores. Data moves between devices by JAX's collectives and lax.ppermute only.
A program may use at most 128 MiB of HBM per device.

v0:
```python
import jax
import jax.numpy as jnp
from jax import lax
from jax.sharding import PartitionSpec as P

coeffs = (
    -5369.0 / 1800.0,
    12.0 / 7.0,
    -15.0 / 56.0,
    10.0 / 189.0,
    -1.0 / 112.0,
    2.0 / 1925.0,
    -1.0 / 16632.0,
)
center_shift = 32.5
half_width = 27.5


def extended_2(cells, sides, width):
    for axis, dim in sides:
        count = lax.axis_size(axis)
        head = lax.slice_in_dim(cells, 0, width, axis=dim)
        tail = lax.slice_in_dim(cells, cells.shape[dim] - width, cells.shape[dim], axis=dim)
        cells = jnp.concatenate(
            [
                lax.ppermute(tail, axis, [(i, (i + 1) % count) for i in range(count)]),
                cells,
                lax.ppermute(head, axis, [((i + 1) % count, i) for i in range(count)]),
            ],
            axis=dim,
        )
    return cells


def apply_ham(extended, pot, width):
    middle = extended[:, 6 : 6 + width]
    lap = 3.0 * coeffs[0] * middle
    for k in range(1, 7):
        lap = lap + coeffs[k] * (
            extended[:, 6 + k : 6 + k + width] + extended[:, 6 - k : 6 - k + width]
        )
    for k in range(1, 7):
        lap = lap + coeffs[k] * (jnp.roll(middle, -k, axis=3) + jnp.roll(middle, k, axis=3))
    depth = middle.shape[2]
    planes_out = []
    for j in range(depth):
        plane = lap[:, :, j]
        for k in range(1, 7):
            if j + k < depth:
                plane = plane + coeffs[k] * middle[:, :, j + k]
            if j - k >= 0:
                plane = plane + coeffs[k] * middle[:, :, j - k]
        planes_out.append(plane)
    lap = jnp.stack(planes_out, axis=2)
    return -2.0 * lap + pot[None] * middle


def plane_rim(field):
    return extended_2(field, (("dom", 1),), 6)


def per_device(psi, potential, rotation):
    planes = psi.shape[1]
    first = (apply_ham(plane_rim(psi), potential, planes) - center_shift * psi) / half_width
    second = (
        2.0 / half_width * (apply_ham(plane_rim(first), potential, planes) - center_shift * first)
        - psi
    )
    filtered = second.astype(jnp.bfloat16)
    own_states = psi.shape[0]
    my_columns = lax.dynamic_slice_in_dim(
        rotation, lax.axis_index("band") * own_states, own_states, 1
    )
    piece = lax.all_gather(filtered, "band", axis=0, tiled=True)
    count = piece.shape[0]
    result = lax.dot_general(
        my_columns,
        piece.reshape(count, -1),
        (((0,), (0,)), ((), ())),
        preferred_element_type=jnp.float32,
    ).astype(jnp.bfloat16)
    return result.reshape(psi.shape)


def solution(mesh):
    in_specs = (P("band", "dom", None, None), P("dom", None, None), P())
    out_specs = P("band", "dom", None, None)
    return jax.shard_map(
        per_device, mesh=mesh, in_specs=in_specs, out_specs=out_specs, check_vma=False
    )
```

profile of v0, /device:TPU:99, one launch (start us, length us, event | category | flops | bytes accessed | tf_op | source)
XLA Modules:
  0.0 579.2 jit_solution(7823604162279824461)
XLA Ops:
  6.5 0.0 copy-start
  6.5 0.0 copy-start.1
  6.5 0.0 all-gather.2.cloned.1.call-start
  6.5 1.8 fusion.79
  8.4 3.8 collective-permute-start.1
  12.1 1.9 collective-permute-start
  14.1 0.0 copy-done.1
  14.1 1.6 fusion.80
  15.7 1.6 fusion.82
  17.3 1.6 fusion.84
  18.9 1.6 fusion.87
  20.5 1.6 fusion.89
  22.1 0.5 fusion.81
  22.6 0.5 fusion.83
  23.2 0.5 fusion.85
  23.7 0.5 fusion.86
  24.2 0.0 copy-start.2
  24.2 0.5 fusion.88
  24.8 0.2 copy-done.2
  25.0 0.5 fusion.90
  25.6 13.2 %fusion.91 = (f32[32,12,2,380]{3,2,1,0:T(2,128)S(1)}, f32[32,12,2,380]{3,2,1,0:T(2,128)S(1)}) fusion(f32[32,12,2,384]{3,2,1,0:T(2,128)S(1)} %copy-done.1), kind=kLoop, calls=%fused_computation.143 | loop fusion | bytes 4669440 | tf_op jit(solution)/shard_map/jit(_roll_static)/slice | solution.py:43
  38.7 0.0 collective-permute-done.1
  38.7 0.2 constant_dynamic-update-slice_fusion.3
  39.0 0.7 constant_dynamic-update-slice_fusion.1
  39.7 0.0 collective-permute-done
  39.7 0.3 constant_dynamic-update-slice_fusion
  40.0 17.1 %fusion.41 = f32[32,12,2,384]{3,2,1,0:T(2,128)S(1)} fusion(f32[32,12,2,4]{3,2,1,0:T(2,128)S(1)} %get-tuple-element.62, f32[32,12,2,380]{3,2,1,0:T(2,128)S(1)} %get-tuple-element.64, f32[32,12,2,380]{3,2,1,0:T(2,128)S(1)} %get-tuple-element.63, f32[32,12,2,4]{3,2,1,0:T(2,128)S(1)} %get-tuple-element.61, f32[32,12,2,5]{3,2,1,0:T(2,128)S(1)} %get-tuple-element.58, ...), kind=kLoop, calls=%fused_computation.74 | loop fusion | flops 14450688 | bytes 30670848 | tf_op jit(solution)/shard_map/add | solution.py:43
  57.1 1.7 slice_add_fusion.7
  58.8 2.0 broadcast_multiply_fusion
  60.8 1.6 fusion.67
  62.4 1.6 fusion.69
  64.0 1.6 fusion.72
  65.6 1.6 fusion.74
  67.2 1.6 fusion.76
  68.8 0.4 fusion.66
  69.2 0.5 fusion.68
  69.7 0.5 fusion.70
  70.3 0.5 fusion.71
  70.8 0.5 fusion.73
  71.3 6.1 %collective-permute-start.2 = (f32[32,6,2,384]{3,2,1,0:T(2,128)S(1)}, f32[32,6,2,384]{3,2,1,0:T(2,128)S(1)}, u32[]{:S(2)}, u32[]{:S(2)}) collective-permute-start(f32[32,6,2,384]{3,2,1,0:T(2,128)S(1)} %get-tuple-element.11), channel_id=1, source_target_pairs={{32,0},{64,32},{96,64},{128,96},{160,128},{192,160},{224,192},{256... | collective-permute-start | bytes 1769480 | tf_op jit(solution)/shard_map/ppermute | solution.py:28
  77.4 2.1 collective-permute-start.3
  79.5 0.5 fusion.75
  80.1 0.5 fusion.77
  80.6 1.6 fusion.78
  82.2 0.3 collective-permute-done.2
  82.5 3.6 collective-permute-done.3
  86.1 18.5 %fusion.52 = f32[32,12,2,384]{3,2,1,0:T(2,128)S(1)} fusion(f32[32,12,2,3]{3,2,1,0:T(2,128)S(1)} %get-tuple-element.34, f32[32,12,2,381]{3,2,1,0:T(2,128)S(1)} %get-tuple-element.36, f32[32,12,2,381]{3,2,1,0:T(2,128)S(1)} %get-tuple-element.35, f32[32,12,2,3]{3,2,1,0:T(2,128)S(1)} %get-tuple-element.33, f32[32,12,2,4]{3,2,1,0:T(2,128)S(1)} %get-tuple-element.30, ...), kind=kLoop, calls=%fused_computation.91 | loop fusion | flops 17989632 | bytes 18874368 | tf_op jit(solution)/shard_map/add | solution.py:43
  104.6 1.7 fusion.62
  106.3 2.9 fusion.60
  109.2 0.0 all-gather.2.cloned.1.call-update
  109.2 422.1 %all-gather.2.cloned.1.call-done = bf16[1024,12,2,384]{3,2,1,0:T(2,128)(2,1)} async-done(((bf16[32,12,2,384]{3,2,1,0:T(2,128)(2,1)}), bf16[1024,12,2,384]{3,2,1,0:T(2,128)(2,1)}) %all-gather.2.cloned.1.call-update) | async-done | bytes 18874384 | tf_op jit(solution)/shard_map/all_gather | solution.py:74
  531.3 29.6 %reshape.7 = bf16[1024,9216]{1,0:T(8,128)(2,1)} reshape(bf16[1024,12,2,384]{3,2,1,0:T(2,128)(2,1)} %all-gather.2.cloned.1.call-done) | data formatting | bytes 37748736 | tf_op jit(solution)/shard_map/reshape | solution.py:78
  560.9 0.0 copy-done
  560.9 9.8 %convolution_convert_fusion = bf16[32,9216]{1,0:T(8,128)(2,1)S(1)} fusion(bf16[1024,9216]{1,0:T(8,128)(2,1)} %reshape.7, bf16[1024,1024]{1,0:T(8,128)(2,1)S(1)} %copy-done, s32[]{:T(128)S(6)} %select_n.3), kind=kOutput, calls=%fused_computation | convolution fusion | flops 604274688 | bytes 19726340 | tf_op jit(solution)/shard_map/dot_general | solution.py:76
  570.7 1.3 reshape.8
  (1 shorter events, 0.0 us)
Async XLA Ops:
  6.5 554.4 %copy-start = (bf16[1024,1024]{1,0:T(8,128)(2,1)S(1)}, bf16[1024,1024]{1,0:T(8,128)(2,1)}, u32[]{:S(2)}) copy-start(bf16[1024,1024]{1,0:T(8,128)(2,1)} %param.5) | copy-start | bytes 6291460
  6.5 7.5 %copy-start.1 = (f32[32,12,2,384]{3,2,1,0:T(2,128)S(1)}, f32[32,12,2,384]{3,2,1,0:T(2,128)}, u32[]{:S(2)}) copy-start(f32[32,12,2,384]{3,2,1,0:T(2,128)} %param.3) | copy-start | bytes 3538948
  6.5 524.7 %all-gather.2.cloned.1.call-start = ((), (), s32[]{:S(2)}) async-start(), calls=%async_computation | async-start | bytes 19464192 | tf_op jit(solution)/shard_map/all_gather | solution.py:74
  8.4 30.4 %collective-permute-start.1 = (f32[32,6,2,384]{3,2,1,0:T(2,128)S(1)}, f32[32,6,2,384]{3,2,1,0:T(2,128)S(1)}, u32[]{:S(2)}, u32[]{:S(2)}) collective-permute-start(f32[32,6,2,384]{3,2,1,0:T(2,128)S(1)} %get-tuple-element.38), channel_id=1, source_target_pairs={{0,32},{32,64},{64,96},{96,128},{128,160},{160,192},{192,224},{224... | collective-permute-start | bytes 1769480 | tf_op jit(solution)/shard_map/ppermute | solution.py:26
  12.1 27.6 %collective-permute-start = (f32[32,6,2,384]{3,2,1,0:T(2,128)S(1)}, f32[32,6,2,384]{3,2,1,0:T(2,128)S(1)}, u32[]{:S(2)}, u32[]{:S(2)}) collective-permute-start(f32[32,6,2,384]{3,2,1,0:T(2,128)S(1)} %get-tuple-element.37), channel_id=1, source_target_pairs={{32,0},{64,32},{96,64},{128,96},{160,128},{192,160},{224,192},{256... | collective-permute-start | bytes 1769480 | tf_op jit(solution)/shard_map/ppermute | solution.py:28
  24.2 0.8 copy-start.2
  71.3 11.2 %collective-permute-start.2 = (f32[32,6,2,384]{3,2,1,0:T(2,128)S(1)}, f32[32,6,2,384]{3,2,1,0:T(2,128)S(1)}, u32[]{:S(2)}, u32[]{:S(2)}) collective-permute-start(f32[32,6,2,384]{3,2,1,0:T(2,128)S(1)} %get-tuple-element.11), channel_id=1, source_target_pairs={{32,0},{64,32},{96,64},{128,96},{160,128},{192,160},{224,192},{256... | collective-permute-start | bytes 1769480 | tf_op jit(solution)/shard_map/ppermute | solution.py:28
  77.4 8.7 %collective-permute-start.3 = (f32[32,6,2,384]{3,2,1,0:T(2,128)S(1)}, f32[32,6,2,384]{3,2,1,0:T(2,128)S(1)}, u32[]{:S(2)}, u32[]{:S(2)}) collective-permute-start(f32[32,6,2,384]{3,2,1,0:T(2,128)S(1)} %get-tuple-element.12), channel_id=1, source_target_pairs={{0,32},{32,64},{64,96},{96,128},{128,160},{160,192},{192,224},{224... | collective-permute-start | bytes 1769480 | tf_op jit(solution)/shard_map/ppermute | solution.py:26
Sparse Core Ops, SparseCore 0:
  109.3 421.9 all-gather.1
where the time goes:
time: 589 us; the launch traced here: 579 us
  waiting for transfers between devices  426 us (72%)
  local copies, waits for them, and re-layouts  71.6 us (12%)
  other arithmetic  43.8 us (7%)
  between operations  14.1 us (2%)
  starting transfers between devices  13.9 us (2%)
  matrix products  9.84 us (2%)
    all_gather x1, waiting for transfers between devices, per_device(): piece = lax.all_gather(filtered, 'band', axis=0, tiled=True)  422 us
    add x2, other arithmetic, apply_ham(): lap + coeffs[k] * (jnp.roll(middle, -k, axis=3) + jnp.roll(middle, k, axi...  35.5 us
    reshape x1, local copies, waits for them, and re-layouts, per_device(): piece.reshape(count, -1)  29.6 us
    slice x14, local copies, waits for them, and re-layouts, apply_ham(): jnp.roll(middle, k, axis=3)  26.4 us
  transfers between devices with their start and end apart: 5, of which 3 were waited for; matrix products, arithmetic and copies ran while one was open for 5% of the time, Pallas kernels for 0%

commit v1 on v0

--- a/solution.py
+++ b/solution.py
@@ -2,6 +2,7 @@
 import jax.numpy as jnp
 from jax import lax
 from jax.sharding import PartitionSpec as P
+from jax.lax import all_to_all, axis_size
 
 coeffs = (
     -5369.0 / 1800.0,
@@ -71,7 +72,9 @@
     my_columns = lax.dynamic_slice_in_dim(
         rotation, lax.axis_index("band") * own_states, own_states, 1
     )
-    piece = lax.all_gather(filtered, "band", axis=0, tiled=True)
+    piece = jnp.concatenate(
+        all_to_all(jnp.stack([filtered] * axis_size("band"), axis=0), "band", 0, 0), axis=0
+    )
     count = piece.shape[0]
     result = lax.dot_general(
         my_columns,

time: 589 us -> 1020 us (1.73)
  the two profiles are of different devices: /device:TPU:99 before, /device:TPU:189 now
where the time goes in v1:
time: 1020 us; the launch traced here: 1010 us
  waiting for transfers between devices  838 us (82%)
  local copies, waits for them, and re-layouts  90.1 us (9%)
  other arithmetic  43.1 us (4%)
  starting transfers between devices  28.2 us (3%)
    all_to_all x1, waiting for transfers between devices, per_device(): all_to_all(jnp.stack([filtered] * axis_size('band'), axis=0), 'band', 0, 0)  834 us
    add x2, other arithmetic, apply_ham(): lap + coeffs[k] * (jnp.roll(middle, -k, axis=3) + jnp.roll(middle, k, axi...  35.5 us
    another operation x1, local copies, waits for them, and re-layouts, per_device(): piece.reshape(count, -1)  29.6 us
    slice x14, local copies, waits for them, and re-layouts, apply_ham(): jnp.roll(middle, k, axis=3)  26.4 us
  transfers between devices with their start and end apart: 5, of which 3 were waited for; matrix products, arithmetic and copies ran while one was open for 3% of the time, Pallas kernels for 0%

profile of v1, /device:TPU:189, one launch (start us, length us, event | category | flops | bytes accessed | tf_op | source)
XLA Modules:
  0.0 1010.1 jit_solution(10941734163354964685)
XLA Ops:
  0.0 0.0 copy-start
  0.0 0.0 copy-start.1
  0.0 1.8 fusion.79
  1.8 2.4 collective-permute-start.1
  4.2 2.1 collective-permute-start
  6.3 0.0 copy-done.1
  6.3 1.6 fusion.80
  8.0 1.6 fusion.82
  9.6 1.6 fusion.84
  11.2 1.6 fusion.87
  12.8 1.6 fusion.89
  14.4 0.5 fusion.81
  14.9 0.5 fusion.83
  15.5 0.5 fusion.85
  16.0 0.5 fusion.86
  16.5 0.0 copy-start.2
  16.5 0.5 fusion.88
  17.1 0.2 copy-done.2
  17.3 0.5 fusion.90
  17.8 13.2 %fusion.91 = (f32[32,12,2,380]{3,2,1,0:T(2,128)S(1)}, f32[32,12,2,380]{3,2,1,0:T(2,128)S(1)}) fusion(f32[32,12,2,384]{3,2,1,0:T(2,128)S(1)} %copy-done.1), kind=kLoop, calls=%fused_computation.143 | loop fusion | bytes 4669440 | tf_op jit(solution)/shard_map/jit(_roll_static)/slice | solution.py:44
  31.0 0.0 collective-permute-done.1
  31.0 0.2 constant_dynamic-update-slice_fusion.3
  31.2 0.7 constant_dynamic-update-slice_fusion.1
  32.0 0.0 collective-permute-done
  32.0 0.3 constant_dynamic-update-slice_fusion
  32.3 17.1 %fusion.41 = f32[32,12,2,384]{3,2,1,0:T(2,128)S(1)} fusion(f32[32,12,2,4]{3,2,1,0:T(2,128)S(1)} %get-tuple-element.62, f32[32,12,2,380]{3,2,1,0:T(2,128)S(1)} %get-tuple-element.64, f32[32,12,2,380]{3,2,1,0:T(2,128)S(1)} %get-tuple-element.63, f32[32,12,2,4]{3,2,1,0:T(2,128)S(1)} %get-tuple-element.61, f32[32,12,2,5]{3,2,1,0:T(2,128)S(1)} %get-tuple-element.58, ...), kind=kLoop, calls=%fused_computation.74 | loop fusion | flops 14450688 | bytes 30670848 | tf_op jit(solution)/shard_map/add | solution.py:44
  49.4 1.7 slice_add_fusion.7
  51.0 2.0 broadcast_multiply_fusion
  53.0 1.6 fusion.67
  54.6 1.6 fusion.69
  56.3 1.6 fusion.72
  57.9 1.6 fusion.74
  59.5 1.6 fusion.76
  61.1 0.4 fusion.66
  61.5 0.5 fusion.68
  62.0 0.5 fusion.70
  62.6 0.5 fusion.71
  63.1 0.5 fusion.73
  63.6 3.6 collective-permute-start.2
  67.3 5.7 collective-permute-start.3
  73.0 0.5 fusion.75
  73.5 0.5 fusion.77
  74.0 1.6 fusion.78
  75.7 2.8 collective-permute-done.2
  78.4 1.2 collective-permute-done.3
  79.6 18.5 %fusion.52 = f32[32,12,2,384]{3,2,1,0:T(2,128)S(1)} fusion(f32[32,12,2,3]{3,2,1,0:T(2,128)S(1)} %get-tuple-element.34, f32[32,12,2,381]{3,2,1,0:T(2,128)S(1)} %get-tuple-element.36, f32[32,12,2,381]{3,2,1,0:T(2,128)S(1)} %get-tuple-element.35, f32[32,12,2,3]{3,2,1,0:T(2,128)S(1)} %get-tuple-element.33, f32[32,12,2,4]{3,2,1,0:T(2,128)S(1)} %get-tuple-element.30, ...), kind=kLoop, calls=%fused_computation.91 | loop fusion | flops 17989632 | bytes 18874368 | tf_op jit(solution)/shard_map/add | solution.py:44
  98.1 1.7 fusion.62
  99.8 2.2 fusion.60
  102.0 18.6 %stack.8 = bf16[32,32,12,2,384]{4,3,2,1,0:T(2,128)(2,1)} broadcast(bf16[32,12,2,384]{3,2,1,0:T(2,128)(2,1)S(1)} %fusion.60), dimensions={1,2,3,4} | broadcast | bytes 19464192 | tf_op jit(solution)/shard_map/stack | solution.py:76
  120.5 14.3 %all-to-all-start = ((bf16[32,32,12,2,384]{4,3,2,1,0:T(2,128)(2,1)}), bf16[32,32,12,2,384]{4,3,2,1,0:T(2,128)(2,1)}, u32[]{:S(2)}, u32[]{:S(2)}) async-start(bf16[32,32,12,2,384]{4,3,2,1,0:T(2,128)(2,1)} %stack.8), calls=%async_computation | async-start | bytes 37748736 | tf_op jit(solution)/shard_map/all_to_all | solution.py:76
  134.9 834.1 %all-to-all-done = bf16[32,32,12,2,384]{4,3,2,1,0:T(2,128)(2,1)} async-done(((bf16[32,32,12,2,384]{4,3,2,1,0:T(2,128)(2,1)}), bf16[32,32,12,2,384]{4,3,2,1,0:T(2,128)(2,1)}, u32[]{:S(2)}, u32[]{:S(2)}) %all-to-all-start) | async-done | bytes 18874400 | tf_op jit(solution)/shard_map/all_to_all | solution.py:76
  969.0 29.6 %reshape_reshape.3 = bf16[1024,9216]{1,0:T(8,128)(2,1)} reshape(bf16[32,32,12,2,384]{4,3,2,1,0:T(2,128)(2,1)} %all-to-all-done) | data formatting | bytes 37748736 | tf_op jit(solution)/shard_map/reshape;reshape | solution.py:81
  998.6 0.0 copy-done
  998.6 9.8 convolution_convert_fusion
  1008.4 1.3 reshape.6
  (1 shorter events, 0.0 us)
Async XLA Ops:
  0.0 998.6 %copy-start = (bf16[1024,1024]{1,0:T(8,128)(2,1)S(1)}, bf16[1024,1024]{1,0:T(8,128)(2,1)}, u32[]{:S(2)}) copy-start(bf16[1024,1024]{1,0:T(8,128)(2,1)} %param.5) | copy-start | bytes 6291460
  0.0 6.3 copy-start.1
  1.8 29.2 %collective-permute-start.1 = (f32[32,6,2,384]{3,2,1,0:T(2,128)S(1)}, f32[32,6,2,384]{3,2,1,0:T(2,128)S(1)}, u32[]{:S(2)}, u32[]{:S(2)}) collective-permute-start(f32[32,6,2,384]{3,2,1,0:T(2,128)S(1)} %get-tuple-element.38), channel_id=1, source_target_pairs={{0,32},{32,64},{64,96},{96,128},{128,160},{160,192},{192,224},{224... | collective-permute-start | bytes 1769480 | tf_op jit(solution)/shard_map/ppermute | solution.py:27
  4.2 27.8 %collective-permute-start = (f32[32,6,2,384]{3,2,1,0:T(2,128)S(1)}, f32[32,6,2,384]{3,2,1,0:T(2,128)S(1)}, u32[]{:S(2)}, u32[]{:S(2)}) collective-permute-start(f32[32,6,2,384]{3,2,1,0:T(2,128)S(1)} %get-tuple-element.37), channel_id=1, source_target_pairs={{32,0},{64,32},{96,64},{128,96},{160,128},{192,160},{224,192},{256... | collective-permute-start | bytes 1769480 | tf_op jit(solution)/shard_map/ppermute | solution.py:29
  16.5 0.8 copy-start.2
  63.6 14.8 %collective-permute-start.2 = (f32[32,6,2,384]{3,2,1,0:T(2,128)S(1)}, f32[32,6,2,384]{3,2,1,0:T(2,128)S(1)}, u32[]{:S(2)}, u32[]{:S(2)}) collective-permute-start(f32[32,6,2,384]{3,2,1,0:T(2,128)S(1)} %get-tuple-element.11), channel_id=1, source_target_pairs={{32,0},{64,32},{96,64},{128,96},{160,128},{192,160},{224,192},{256... | collective-permute-start | bytes 1769480 | tf_op jit(solution)/shard_map/ppermute | solution.py:29
  67.3 12.3 %collective-permute-start.3 = (f32[32,6,2,384]{3,2,1,0:T(2,128)S(1)}, f32[32,6,2,384]{3,2,1,0:T(2,128)S(1)}, u32[]{:S(2)}, u32[]{:S(2)}) collective-permute-start(f32[32,6,2,384]{3,2,1,0:T(2,128)S(1)} %get-tuple-element.12), channel_id=1, source_target_pairs={{0,32},{32,64},{64,96},{96,128},{128,160},{160,192},{192,224},{224... | collective-permute-start | bytes 1769480 | tf_op jit(solution)/shard_map/ppermute | solution.py:27
  120.5 848.5 %all-to-all-start = ((bf16[32,32,12,2,384]{4,3,2,1,0:T(2,128)(2,1)}), bf16[32,32,12,2,384]{4,3,2,1,0:T(2,128)(2,1)}, u32[]{:S(2)}, u32[]{:S(2)}) async-start(bf16[32,32,12,2,384]{4,3,2,1,0:T(2,128)(2,1)} %stack.8), calls=%async_computation | async-start | bytes 37748736 | tf_op jit(solution)/shard_map/all_to_all | solution.py:76
